TPU v7x, 512 devices: a whole 4x4x16 slice. The times are simulated.
512 devices in a mesh: row: 32 (over y, x, core), col: 16 (over z).
Axes of the slice: x: 4, y: 4, z: 16, core: 2. Of those that a mesh axis runs over, the one named last changes fastest.
Arguments:
- queries: bfloat16 [512, 16, 1024], P('row', None, 'col'), may hold values from -30 to 30
- new_keys: bfloat16 [512, 1024], P('row', 'col'), may hold values from -6 to 6
- new_values: bfloat16 [512, 1024], P('row', 'col'), may hold values from -12 to 12
- cache_keys: bfloat16 [512, 128, 1024], P('row', None, 'col'), may hold values from -8 to 8
- cache_values: bfloat16 [512, 128, 1024], P('row', None, 'col'), may hold values from -12 to 12
- lengths: int32 [512], P('row'), may hold values from 64 to 128
- parents: int32 [512], P('row'), may hold values from 0 to 511, as said below
- residual: bfloat16 [512, 16, 1024], P('row', None, 'col'), may hold values from -20 to 20
- norm_gain: bfloat16 [16, 1024], P(None, 'col'), may hold values from 0.5 to 1.5
- vocab_weight: bfloat16 [16, 1024, 64128], P(None, 'col', 'row')
Outputs:
- logprobs: float32 [512, 64128], P('col', 'row')
Inputs may be any that keep to these rules, and one draw needn't show every extreme that they name: Among the 16 child beams of one index of row, at most 2 have their parents on the beams of any single index of row, and exactly 2 do for some index.
All inputs are finite; a program needn't handle non-finite values.
Results may differ from a plain program's by a relative error of at most 0.0015.
Values may be sent and summed in bfloat16 or wider, within the bound.
No kernel may reach another device: no remote copies, remote signals or barrier semaphores. Data moves between devices by JAX's collectives and lax.ppermute only.
A program may use at most 64 MiB of HBM per device.

v0:
```python
import jax
import jax.numpy as jnp
from jax import lax
from jax.sharding import PartitionSpec as P

HEAD_DIM = 128
D = 16384


def from_partner(value, axis, distance):
    mask = 2**distance
    pairs = [(source, source ^ mask) for source in range(lax.axis_size(axis))]
    return lax.ppermute(value, axis, pairs)


def count_before(sources):
    entries = sources.shape[-1]
    earlier = jnp.arange(entries)[:, None] > jnp.arange(entries)[None, :]
    matching = sources[..., :, None] == sources[..., None, :]
    return jnp.sum(matching & earlier, axis=-1)


def attend(queries_in, key_cache, value_cache, key_new, value_new, live_rows):
    leading = queries_in.shape[:-2]
    group_size = queries_in.shape[-2]
    panel_width = queries_in.shape[-1]
    head_part = min(panel_width, HEAD_DIM)
    heads_here = panel_width // head_part
    context = key_cache.shape[-2]
    query_heads = queries_in.reshape(leading + (group_size, heads_here, head_part))
    key_heads = key_cache.reshape(leading + (context, heads_here, head_part))
    value_heads = value_cache.reshape(leading + (context, heads_here, head_part))
    fresh_key = key_new.reshape(leading + (heads_here, head_part))
    fresh_value = value_new.reshape(leading + (1, heads_here, head_part)).astype(jnp.float32)
    cached = jnp.einsum(
        "...jhe,...the->...jht", query_heads, key_heads, preferred_element_type=jnp.float32
    )
    own_score = jnp.einsum(
        "...jhe,...he->...jh", query_heads, fresh_key, preferred_element_type=jnp.float32
    )
    other_cached, other_own = from_partner((cached, own_score), "col", 0)
    cached = cached + other_cached
    own_score = own_score + other_own
    scale_factor = HEAD_DIM ** (-0.5)
    cached = cached * scale_factor
    own_score = own_score * scale_factor
    positions = lax.broadcasted_iota(jnp.int32, cached.shape, cached.ndim - 1)
    visible = positions < live_rows.reshape(leading + (1, 1, 1))
    peak_score = jnp.maximum(jnp.max(jnp.where(visible, cached, -jnp.inf), axis=-1), own_score)
    weight = jnp.where(visible, jnp.exp(cached - peak_score[..., None]), jnp.float32(0.0))
    weight_own = jnp.exp(own_score - peak_score)
    weight_sum = jnp.sum(weight, axis=-1) + weight_own
    rounded = weight.astype(jnp.bfloat16)
    rounded_own = lax.optimization_barrier(weight_own.astype(jnp.bfloat16)).astype(jnp.float32)
    summed = jnp.einsum(
        "...jht,...the->...jhe", rounded, value_heads, preferred_element_type=jnp.float32
    )
    own_part = rounded_own[..., None] * fresh_value
    result = (summed + own_part) / weight_sum[..., None]
    return result.reshape(leading + (group_size, panel_width)).astype(jnp.bfloat16)


def body(
    queries,
    new_keys,
    new_values,
    cache_keys,
    cache_values,
    lengths,
    parents,
    residual,
    norm_gain,
    vocab_weight,
):
    row_count = lax.axis_size("row")
    beam_count = parents.shape[0]
    slot_cap = max(2, (2 * beam_count + row_count - 1) // row_count)
    my_row = lax.axis_index("row")
    group_size = queries.shape[1]
    panel_width = queries.shape[2]
    source = parents // beam_count
    rank_in = count_before(source)
    slot_index = source * slot_cap + rank_in
    slot_range = jnp.arange(slot_cap, dtype=jnp.int32)
    all_parents, all_lengths = (
        lax.all_gather(parents, "row", axis=0, tiled=True),
        lax.all_gather(lengths, "row", axis=0, tiled=True),
    )
    parent_table = all_parents.reshape(row_count, beam_count)
    sources_all = parent_table // beam_count
    offsets_all = parent_table % beam_count
    ranks_all = count_before(sources_all)
    chosen = (sources_all[:, None, :] == my_row) & (
        ranks_all[:, None, :] == slot_range[None, :, None]
    )
    rows_sent = jnp.sum(jnp.where(chosen, offsets_all[:, None, :], 0), axis=2)
    got_keys, got_values = (
        lax.all_to_all(cache_keys[rows_sent], "row", split_axis=0, concat_axis=0, tiled=True),
        lax.all_to_all(cache_values[rows_sent], "row", split_axis=0, concat_axis=0, tiled=True),
    )
    context = cache_keys.shape[1]
    kept_keys = got_keys.reshape(row_count * slot_cap, context, panel_width)[slot_index]
    kept_values = got_values.reshape(row_count * slot_cap, context, panel_width)[slot_index]
    attended = attend(queries, kept_keys, kept_values, new_keys, new_values, all_lengths[parents])
    stream = residual.astype(jnp.float32) + attended.astype(jnp.float32)
    square_sums = lax.psum(jnp.sum(stream * stream, axis=(1, 2)), "col")
    scaling = lax.rsqrt(square_sums / D + 1e-05)
    normed = (stream * norm_gain.astype(jnp.float32)[None] * scaling[:, None, None]).astype(
        jnp.bfloat16
    )
    gathered = lax.all_gather(normed, "row", axis=0, tiled=True)
    flat_rows = gathered.reshape(gathered.shape[0], group_size * panel_width)
    flat_weight = vocab_weight.reshape(group_size * panel_width, vocab_weight.shape[2])
    logits = lax.psum_scatter(
        jnp.dot(flat_rows, flat_weight, preferred_element_type=jnp.float32),
        "col",
        scatter_dimension=0,
        tiled=True,
    )
    totals = lax.psum(jnp.sum(jnp.exp(logits), axis=1), "row")
    return logits - jnp.log(totals)[:, None]


def solution(mesh):
    placed = (
        P("row", None, "col"),
        P("row", "col"),
        P("row", "col"),
        P("row", None, "col"),
        P("row", None, "col"),
        P("row"),
        P("row"),
        P("row", None, "col"),
        P(None, "col"),
        P(None, "col", "row"),
    )
    return jax.shard_map(
        body, mesh=mesh, in_specs=placed, out_specs=P("col", "row"), check_vma=False
    )
```

profile of v0, /device:TPU:1, one launch (start us, length us, event | category | flops | bytes accessed | tf_op | source)
XLA Modules:
  0.0 322.9 jit_solution(3743280184073839747)
XLA Ops:
  6.5 0.0 copy-start
  6.5 1.3 dynamic-slice
  8.5 0.9 dynamic-update-slice
  9.4 0.8 dynamic-update-slice.1
  10.2 14.4 %all-reduce.2 = (s32[512]{0:T(512)S(1)}, s32[512]{0:T(512)S(1)}) all-reduce(s32[512]{0:T(512)S(1)} %dynamic-update-slice, s32[512]{0:T(512)S(1)} %dynamic-update-slice.1), channel_id=1, replica_groups=mesh['row'=32,'col'=16] {'row'}, use_global_device_ids=true, to_apply=%add | all-reduce | flops 1024 | bytes 8192
  24.7 0.1 reshape.188
  24.7 0.1 copy.23
  24.8 0.1 convert_reduce_fusion
  25.0 0.1 copy.27
  25.1 0.1 reshape.196
  25.2 0.0 copy-done
  25.2 1.7 gather_fusion.3
  26.9 0.0 copy-start.1
  26.9 11.0 %all-to-all-start.1 = ((bf16[32,2,128,64]{2,3,1,0:T(8,128)(2,1)}), bf16[32,2,128,64]{2,3,1,0:T(8,128)(2,1)S(1)}, u32[]{:S(2)}, u32[]{:S(2)}) async-start(bf16[32,2,128,64]{2,3,1,0:T(8,128)(2,1)} %bitcast.4), calls=%async_computation.1 | async-start | bytes 2097152 | tf_op jit(solution)/shard_map/all_to_all | solution.py:98
  37.9 0.0 copy-done.1
  37.9 1.7 gather_fusion
  39.6 0.0 copy-start.7
  39.6 0.0 copy-start.2
  39.6 0.0 copy-start.6
  39.6 0.0 copy-start.3
  39.6 0.0 copy-start.4
  39.6 15.3 %all-to-all-done.1 = bf16[32,2,128,64]{2,3,1,0:T(8,128)(2,1)S(1)} async-done(((bf16[32,2,128,64]{2,3,1,0:T(8,128)(2,1)}), bf16[32,2,128,64]{2,3,1,0:T(8,128)(2,1)S(1)}, u32[]{:S(2)}, u32[]{:S(2)}) %all-to-all-start.1) | async-done | bytes 1048608 | tf_op jit(solution)/shard_map/all_to_all | solution.py:98
  54.9 4.0 %all-to-all-start = ((bf16[32,2,128,64]{2,3,1,0:T(8,128)(2,1)}), bf16[32,2,128,64]{2,3,1,0:T(8,128)(2,1)S(1)}, u32[]{:S(2)}, u32[]{:S(2)}) async-start(bf16[32,2,128,64]{2,3,1,0:T(8,128)(2,1)} %bitcast.2), calls=%async_computation | async-start | bytes 2097152 | tf_op jit(solution)/shard_map/all_to_all | solution.py:99
  58.9 0.0 copy-start.5
  58.9 0.0 all-gather.2.cloned.1.call-start
  59.0 0.0 copy-done.7
  59.0 0.2 convert_reduce_fusion.1
  59.2 0.6 gather_fusion.4
  59.8 0.0 copy-done.2
  59.8 0.2 convolution_bitcast_fusion.1
  60.0 1.9 collective-permute-start
  61.9 0.0 copy-done.6
  61.9 0.1 fusion.16
  62.1 3.4 %collective-permute-start.1 = (f32[16,16,1]{1,0,2:T(8,128)S(1)}, f32[16,16,1]{1,0,2:T(8,128)S(1)}, u32[]{:S(2)}, u32[]{:S(2)}) collective-permute-start(f32[16,16,1]{1,0,2:T(8,128)S(1)} %bitcast.75), channel_id=1, source_target_pairs={{0,1},{1,0},{2,3},{3,2},{4,5},{5,4},{6,7},{7,6},{8,9},{9,8},{10,11... | collective-permute-start | bytes 3080 | tf_op jit(solution)/shard_map/ppermute | solution.py:13
  65.5 0.0 copy-done.3
  65.5 0.0 copy-done.4
  65.5 0.7 gather_fusion.2
  66.2 9.9 %all-to-all-done = bf16[32,2,128,64]{2,3,1,0:T(8,128)(2,1)S(1)} async-done(((bf16[32,2,128,64]{2,3,1,0:T(8,128)(2,1)}), bf16[32,2,128,64]{2,3,1,0:T(8,128)(2,1)S(1)}, u32[]{:S(2)}, u32[]{:S(2)}) %all-to-all-start) | async-done | bytes 1048608 | tf_op jit(solution)/shard_map/all_to_all | solution.py:99
  76.1 0.6 gather_fusion.1
  76.7 0.0 collective-permute-done
  76.7 0.2 select_reduce_fusion
  76.9 0.0 collective-permute-done.1
  76.9 0.2 fusion.7
  77.1 0.0 copy-done.5
  77.2 0.4 multiply_reduce_fusion
  77.6 26.0 %psum.14 = f32[16]{0:T(128)S(1)} all-reduce(f32[16]{0:T(128)S(1)} %get-tuple-element.13), channel_id=1, replica_groups=mesh['row'=32,'col'=16] {'col'}, use_global_device_ids=true, to_apply=%region_6.7 | all-reduce | flops 16 | bytes 128 | tf_op jit(solution)/shard_map/psum | solution.py:106
  103.6 0.7 multiply_convert_fusion
  104.4 0.0 all-gather.2.cloned.1.call-update
  104.4 0.0 reduce-scatter.2.cloned.1.call-start
  104.4 58.6 %all-gather.2.cloned.1.call-done = bf16[512,16,64]{2,1,0:T(8,128)(2,1)} async-done(((bf16[16,16,64]{2,1,0:T(8,128)(2,1)}), bf16[512,16,64]{2,1,0:T(8,128)(2,1)}) %all-gather.2.cloned.1.call-update) | async-done | bytes 1048592 | tf_op jit(solution)/shard_map/all_gather | solution.py:111
  163.0 7.4 %convolution_bitcast_fusion = f32[512,2004]{1,0:T(8,128)} fusion(bf16[16,64,2004]{2,1,0:T(8,128)(2,1)} %param.19, bf16[512,16,64]{2,1,0:T(8,128)(2,1)} %all-gather.2.cloned.1.call-done), kind=kOutput, calls=%fused_computation.5 | convolution fusion | flops 2101346304 | bytes 9256960 | tf_op jit(solution)/shard_map/dot_general | solution.py:115
  170.4 0.0 reduce-scatter.2.cloned.1.call-update
  170.5 69.5 %reduce-scatter.2.cloned.1.call-done = f32[32,2004]{1,0:T(8,128)} async-done(((f32[512,2004]{1,0:T(8,128)}), f32[32,2004]{1,0:T(8,128)}) %reduce-scatter.2.cloned.1.call-update) | async-done | bytes 256528 | tf_op jit(solution)/shard_map/reduce_scatter | solution.py:114
  240.0 1.1 exponential_reduce_fusion
  241.1 73.2 %psum.15 = f32[32]{0:T(128)S(1)} all-reduce(f32[32]{0:T(128)S(1)} %exponential_reduce_fusion), channel_id=1, replica_groups=mesh['row'=32,'col'=16] {'row'}, use_global_device_ids=true, to_apply=%region_9.10 | all-reduce | flops 32 | bytes 256 | tf_op jit(solution)/shard_map/psum | solution.py:120
  314.3 1.7 broadcast_subtract_fusion
  (19 shorter events, 0.2 us)
Async XLA Ops:
  6.5 18.7 %copy-start = (bf16[16,128,64]{1,2,0:T(8,128)(2,1)S(1)}, bf16[16,128,64]{1,2,0:T(8,128)(2,1)}, u32[]{:S(2)}) copy-start(bf16[16,128,64]{1,2,0:T(8,128)(2,1)} %param.13) | copy-start | bytes 786436
  26.9 11.0 %copy-start.1 = (bf16[16,128,64]{1,2,0:T(8,128)(2,1)S(1)}, bf16[16,128,64]{1,2,0:T(8,128)(2,1)}, u32[]{:S(2)}) copy-start(bf16[16,128,64]{1,2,0:T(8,128)(2,1)} %param.14) | copy-start | bytes 786436
  26.9 28.1 %all-to-all-start.1 = ((bf16[32,2,128,64]{2,3,1,0:T(8,128)(2,1)}), bf16[32,2,128,64]{2,3,1,0:T(8,128)(2,1)S(1)}, u32[]{:S(2)}, u32[]{:S(2)}) async-start(bf16[32,2,128,64]{2,3,1,0:T(8,128)(2,1)} %bitcast.4), calls=%async_computation.1 | async-start | bytes 2097152 | tf_op jit(solution)/shard_map/all_to_all | solution.py:98
  39.6 19.4 %copy-start.7 = (s32[16]{0:T(128)S(1)}, s32[16]{0:T(128)}, u32[]{:S(2)}) copy-start(s32[16]{0:T(128)} %param.16) | copy-start | bytes 196
  39.6 20.2 %copy-start.2 = (bf16[16,16,64]{2,1,0:T(8,128)(2,1)S(1)}, bf16[16,16,64]{2,1,0:T(8,128)(2,1)}, u32[]{:S(2)}) copy-start(bf16[16,16,64]{2,1,0:T(8,128)(2,1)} %param.10) | copy-start | bytes 98308
  39.6 22.3 %copy-start.6 = (bf16[16,64]{1,0:T(8,128)(2,1)S(1)}, bf16[16,64]{1,0:T(8,128)(2,1)}, u32[]{:S(2)}) copy-start(bf16[16,64]{1,0:T(8,128)(2,1)} %param.11) | copy-start | bytes 6148
  39.6 25.8 %copy-start.3 = (bf16[16,64]{1,0:T(8,128)(2,1)S(1)}, bf16[16,64]{1,0:T(8,128)(2,1)}, u32[]{:S(2)}) copy-start(bf16[16,64]{1,0:T(8,128)(2,1)} %param.12) | copy-start | bytes 6148
  39.6 25.9 %copy-start.4 = (bf16[16,64]{1,0:T(8,128)(2,1)S(1)}, bf16[16,64]{1,0:T(8,128)(2,1)}, u32[]{:S(2)}) copy-start(bf16[16,64]{1,0:T(8,128)(2,1)} %param.18) | copy-start | bytes 6148
  54.9 21.1 %all-to-all-start = ((bf16[32,2,128,64]{2,3,1,0:T(8,128)(2,1)}), bf16[32,2,128,64]{2,3,1,0:T(8,128)(2,1)S(1)}, u32[]{:S(2)}, u32[]{:S(2)}) async-start(bf16[32,2,128,64]{2,3,1,0:T(8,128)(2,1)} %bitcast.2), calls=%async_computation | async-start | bytes 2097152 | tf_op jit(solution)/shard_map/all_to_all | solution.py:99
  58.9 18.2 %copy-start.5 = (bf16[16,16,64]{2,1,0:T(8,128)(2,1)S(1)}, bf16[16,16,64]{2,1,0:T(8,128)(2,1)}, u32[]{:S(2)}) copy-start(bf16[16,16,64]{2,1,0:T(8,128)(2,1)} %param.17) | copy-start | bytes 98308
  58.9 104.1 %all-gather.2.cloned.1.call-start = ((), (), s32[]{:S(2)}) async-start(), calls=%async_computation.3 | async-start | bytes 2162688 | tf_op jit(solution)/shard_map/all_gather | solution.py:111
  60.0 16.7 %collective-permute-start = (f32[16,16,1,128]{3,1,0,2:T(8,128)S(1)}, f32[16,16,1,128]{3,1,0,2:T(8,128)S(1)}, u32[]{:S(2)}, u32[]{:S(2)}) collective-permute-start(f32[16,16,1,128]{3,1,0,2:T(8,128)S(1)} %convolution_bitcast_fusion.1), channel_id=1, source_target_pairs={{0,1},{1,0},{2,3},{3,2},{4,5},{5,4},{6,7},{7,6},{8,9},{9,8},{10,11... | collective-permute-start | bytes 393224 | tf_op jit(solution)/shard_map/ppermute | solution.py:13
  62.1 14.8 %collective-permute-start.1 = (f32[16,16,1]{1,0,2:T(8,128)S(1)}, f32[16,16,1]{1,0,2:T(8,128)S(1)}, u32[]{:S(2)}, u32[]{:S(2)}) collective-permute-start(f32[16,16,1]{1,0,2:T(8,128)S(1)} %bitcast.75), channel_id=1, source_target_pairs={{0,1},{1,0},{2,3},{3,2},{4,5},{5,4},{6,7},{7,6},{8,9},{9,8},{10,11... | collective-permute-start | bytes 3080 | tf_op jit(solution)/shard_map/ppermute | solution.py:13
  104.4 135.6 %reduce-scatter.2.cloned.1.call-start = ((), (), s32[]{:S(2)}) async-start(), calls=%async_computation.4 | async-start | bytes 4456448 | tf_op jit(solution)/shard_map/reduce_scatter | solution.py:114
Sparse Core Ops, SparseCore 0:
  104.5 58.4 all-gather.1
  170.6 69.3 reduce-scatter.1
where the time goes:
time: 323 us
  waiting for transfers between devices  153 us (47%)
  blocking collectives  114 us (35%)
  starting transfers between devices  20.3 us (6%)
  between operations  14.3 us (4%)
  local copies, waits for them, and re-layouts  8.63 us (3%)
  matrix products  8.17 us (3%)
  other arithmetic  4.38 us (1%)
    psum x1, blocking collectives, body(): totals = lax.psum(jnp.sum(jnp.exp(logits), axis=1), 'row')  73.2 us
    reduce_scatter x1, waiting for transfers between devices, body(): lax.psum_scatter(jnp.dot(flat_rows, flat_weight, preferred_element_type=j...  69.5 us
    all_gather x1, waiting for transfers between devices, body(): gathered = lax.all_gather(normed, 'row', axis=0, tiled=True)  58.6 us
    psum x1, blocking collectives, body(): square_sums = lax.psum(jnp.sum(stream * stream, axis=(1, 2)), 'col')  26 us
    all_to_all x1, waiting for transfers between devices, body(): lax.all_to_all(cache_keys[rows_sent], 'row', split_axis=0, concat_axis=0,...  15.3 us
    unnamed x1, blocking collectives  14.4 us
    all_to_all x1, starting transfers between devices, body(): lax.all_to_all(cache_keys[rows_sent], 'row', split_axis=0, concat_axis=0,...  11 us
    all_to_all x1, waiting for transfers between devices, body(): lax.all_to_all(cache_values[rows_sent], 'row', split_axis=0, concat_axis=...  9.9 us
  transfers between devices with their start and end apart: 6, of which 4 were waited for; matrix products, arithmetic and copies ran while one was open for 1% of the time, Pallas kernels for 0%

commit v1 on v0

--- a/solution.py
+++ b/solution.py
@@ -5,6 +5,12 @@
 
 HEAD_DIM = 128
 D = 16384
+
+
+def quarters_measure(patch):
+    ready = jnp.stack([patch for _ in range(lax.axis_size("row"))], 0)
+    local_out = lax.all_to_all(ready, "row", 0, 0)
+    return jnp.concatenate(local_out, 0)
 
 
 def from_partner(value, axis, distance):
@@ -108,7 +114,7 @@
     normed = (stream * norm_gain.astype(jnp.float32)[None] * scaling[:, None, None]).astype(
         jnp.bfloat16
     )
-    gathered = lax.all_gather(normed, "row", axis=0, tiled=True)
+    gathered = quarters_measure(normed)
     flat_rows = gathered.reshape(gathered.shape[0], group_size * panel_width)
     flat_weight = vocab_weight.reshape(group_size * panel_width, vocab_weight.shape[2])
     logits = lax.psum_scatter(

time: 323 us -> 292 us (0.904)
  waiting for transfers between devices: 153 us -> 88 us
  blocking collectives: 114 us -> 142 us
  local copies, waits for them, and re-layouts: 8.63 us -> 15.8 us
    all_gather x1 -> x0, waiting for transfers between devices: 58.6 us -> none  [body(): gathered = lax.all_gather(normed, 'row', axis=0, tiled=True)]
    all_to_all x0 -> x1, blocking collectives: none -> 28.1 us  [quarters_measure(): local_out = lax.all_to_all(ready, 'row', 0, 0)]
    reduce_scatter x1, waiting for transfers between devices: 69.5 us -> 62.8 us  [body(): lax.psum_scatter(jnp.dot(flat_rows, flat_weight, preferred_element_type=j...]
    unnamed x21 -> x23, local copies, waits for them, and re-layouts: 3.04 us -> 8.29 us
  transfers between devices with their start and end apart: 6 -> 5, of which waited for: 4 -> 3; matrix products, arithmetic and copies ran while one was open for 1% -> 1% of each run, Pallas kernels for 0% -> 0%
where the time goes in v1:
time: 292 us; the launch traced here: 291 us
  blocking collectives  142 us (49%)
  waiting for transfers between devices  88 us (30%)
  starting transfers between devices  20.3 us (7%)
  local copies, waits for them, and re-layouts  15.8 us (5%)
  between operations  14.4 us (5%)
  matrix products  7.2 us (2%)
  other arithmetic  3.75 us (1%)
    psum x1, blocking collectives, body(): totals = lax.psum(jnp.sum(jnp.exp(logits), axis=1), 'row')  73.1 us
    reduce_scatter x1, waiting for transfers between devices, body(): lax.psum_scatter(jnp.dot(flat_rows, flat_weight, preferred_element_type=j...  62.8 us
    all_to_all x1, blocking collectives, quarters_measure(): local_out = lax.all_to_all(ready, 'row', 0, 0)  28.1 us
    psum x1, blocking collectives, body(): square_sums = lax.psum(jnp.sum(stream * stream, axis=(1, 2)), 'col')  26 us
    all_to_all x1, waiting for transfers between devices, body(): lax.all_to_all(cache_keys[rows_sent], 'row', split_axis=0, concat_axis=0,...  15.3 us
    unnamed x1, blocking collectives  14.4 us
    all_to_all x1, starting transfers between devices, body(): lax.all_to_all(cache_keys[rows_sent], 'row', split_axis=0, concat_axis=0,...  11 us
    all_to_all x1, waiting for transfers between devices, body(): lax.all_to_all(cache_values[rows_sent], 'row', split_axis=0, concat_axis=...  9.91 us
  transfers between devices with their start and end apart: 5, of which 3 were waited for; matrix products, arithmetic and copies ran while one was open for 1% of the time, Pallas kernels for 0%

profile of v1, /device:TPU:1, one launch (start us, length us, event | category | flops | bytes accessed | tf_op | source)
XLA Modules:
  0.0 291.1 jit_solution(15505381573584767959)
XLA Ops:
  6.5 0.0 copy-start
  6.5 0.0 copy-start.1
  6.6 1.3 dynamic-slice
  8.5 0.9 dynamic-update-slice
  9.4 0.8 dynamic-update-slice.1
  10.2 14.4 %all-reduce.2 = (s32[512]{0:T(512)S(1)}, s32[512]{0:T(512)S(1)}) all-reduce(s32[512]{0:T(512)S(1)} %dynamic-update-slice, s32[512]{0:T(512)S(1)} %dynamic-update-slice.1), channel_id=1, replica_groups=mesh['row'=32,'col'=16] {'row'}, use_global_device_ids=true, to_apply=%add | all-reduce | flops 1024 | bytes 8192
  24.7 0.1 reshape.191
  24.8 0.1 copy.18
  24.9 0.1 convert_reduce_fusion
  25.0 0.1 copy.22
  25.1 0.1 reshape.200
  25.2 0.0 copy-done
  25.2 1.7 gather_fusion.3
  26.9 0.0 copy-start.7
  26.9 11.0 %all-to-all-start.1 = ((bf16[32,2,128,64]{2,3,1,0:T(8,128)(2,1)}), bf16[32,2,128,64]{2,3,1,0:T(8,128)(2,1)S(1)}, u32[]{:S(2)}, u32[]{:S(2)}) async-start(bf16[32,2,128,64]{2,3,1,0:T(8,128)(2,1)} %bitcast.4), calls=%async_computation.1 | async-start | bytes 2097152 | tf_op jit(solution)/shard_map/all_to_all | solution.py:104
  37.9 0.0 copy-done.1
  37.9 0.0 copy-start.2
  37.9 0.0 copy-start.6
  38.0 0.0 copy-start.3
  38.0 0.0 copy-start.4
  38.0 0.0 copy-start.5
  38.0 1.7 gather_fusion
  39.7 15.3 %all-to-all-done.1 = bf16[32,2,128,64]{2,3,1,0:T(8,128)(2,1)S(1)} async-done(((bf16[32,2,128,64]{2,3,1,0:T(8,128)(2,1)}), bf16[32,2,128,64]{2,3,1,0:T(8,128)(2,1)S(1)}, u32[]{:S(2)}, u32[]{:S(2)}) %all-to-all-start.1) | async-done | bytes 1048608 | tf_op jit(solution)/shard_map/all_to_all | solution.py:104
  55.0 4.0 %all-to-all-start = ((bf16[32,2,128,64]{2,3,1,0:T(8,128)(2,1)}), bf16[32,2,128,64]{2,3,1,0:T(8,128)(2,1)S(1)}, u32[]{:S(2)}, u32[]{:S(2)}) async-start(bf16[32,2,128,64]{2,3,1,0:T(8,128)(2,1)} %bitcast.2), calls=%async_computation | async-start | bytes 2097152 | tf_op jit(solution)/shard_map/all_to_all | solution.py:105
  59.0 0.0 reduce-scatter.2.cloned.1.call-start
  59.0 0.0 copy-done.7
  59.0 0.2 convert_reduce_fusion.1
  59.2 0.6 gather_fusion.4
  59.8 0.0 copy-done.2
  59.8 0.2 convolution_bitcast_fusion
  60.0 1.9 collective-permute-start
  62.0 0.0 copy-done.6
  62.0 0.1 fusion.15
  62.1 3.4 %collective-permute-start.1 = (f32[16,16,1]{1,0,2:T(8,128)S(1)}, f32[16,16,1]{1,0,2:T(8,128)S(1)}, u32[]{:S(2)}, u32[]{:S(2)}) collective-permute-start(f32[16,16,1]{1,0,2:T(8,128)S(1)} %bitcast.77), channel_id=1, source_target_pairs={{0,1},{1,0},{2,3},{3,2},{4,5},{5,4},{6,7},{7,6},{8,9},{9,8},{10,11... | collective-permute-start | bytes 3080 | tf_op jit(solution)/shard_map/ppermute | solution.py:19
  65.5 0.0 copy-done.3
  65.5 0.0 copy-done.4
  65.5 0.7 gather_fusion.2
  66.2 9.9 %all-to-all-done = bf16[32,2,128,64]{2,3,1,0:T(8,128)(2,1)S(1)} async-done(((bf16[32,2,128,64]{2,3,1,0:T(8,128)(2,1)}), bf16[32,2,128,64]{2,3,1,0:T(8,128)(2,1)S(1)}, u32[]{:S(2)}, u32[]{:S(2)}) %all-to-all-start) | async-done | bytes 1048608 | tf_op jit(solution)/shard_map/all_to_all | solution.py:105
  76.1 0.6 gather_fusion.1
  76.7 0.0 collective-permute-done
  76.7 0.2 select_reduce_fusion
  76.9 0.0 collective-permute-done.1
  76.9 0.2 fusion.6
  77.2 0.0 copy-done.5
  77.2 0.4 multiply_reduce_fusion
  77.6 26.0 %psum.14 = f32[16]{0:T(128)S(1)} all-reduce(f32[16]{0:T(128)S(1)} %get-tuple-element.13), channel_id=1, replica_groups=mesh['row'=32,'col'=16] {'col'}, use_global_device_ids=true, to_apply=%region_6.7 | all-reduce | flops 16 | bytes 128 | tf_op jit(solution)/shard_map/psum | solution.py:112
  103.7 0.1 multiply_convert_fusion
  103.8 0.5 stack.2
  104.2 1.5 reshape.255
  105.7 28.1 %all_to_all.15 = bf16[32,2,8192]{2,1,0:T(2,128)(2,1)} all-to-all(bf16[32,2,8192]{2,1,0:T(2,128)(2,1)S(1)} %reshape.255), channel_id=1, replica_groups=mesh['row'=32,'col'=16] {'row'}, dimensions={0} | all-to-all | bytes 2097152 | tf_op jit(solution)/shard_map/all_to_all | solution.py:12
  133.9 3.8 %reshape.256 = bf16[32,16,16,64]{3,2,1,0:T(8,128)(2,1)S(1)} reshape(bf16[32,2,8192]{2,1,0:T(2,128)(2,1)} %all_to_all.15) | data formatting | bytes 2097152
  137.6 1.5 reshape_reshape.3
  139.1 6.5 %fusion.22 = f32[512,2004]{1,0:T(8,128)} fusion(bf16[512,1024]{1,0:T(8,128)(2,1)S(1)} %reshape_reshape.3, bf16[1024,2004]{1,0:T(8,128)(2,1)} %bitcast.80), kind=kOutput, calls=%fused_computation.64 | convolution fusion | flops 2101346304 | bytes 9256960 | tf_op jit(solution)/shard_map/dot_general | solution.py:121
  145.6 0.0 reduce-scatter.2.cloned.1.call-update
  145.6 62.8 %reduce-scatter.2.cloned.1.call-done = f32[32,2004]{1,0:T(8,128)} async-done(((f32[512,2004]{1,0:T(8,128)}), f32[32,2004]{1,0:T(8,128)}) %reduce-scatter.2.cloned.1.call-update) | async-done | bytes 256528 | tf_op jit(solution)/shard_map/reduce_scatter | solution.py:120
  208.4 1.1 exponential_reduce_fusion
  209.5 73.1 %psum.15 = f32[32]{0:T(128)S(1)} all-reduce(f32[32]{0:T(128)S(1)} %exponential_reduce_fusion), channel_id=1, replica_groups=mesh['row'=32,'col'=16] {'row'}, use_global_device_ids=true, to_apply=%region_9.10 | all-reduce | flops 32 | bytes 256 | tf_op jit(solution)/shard_map/psum | solution.py:126
  282.5 1.7 broadcast_subtract_fusion
  (19 shorter events, 0.2 us)
Async XLA Ops:
  6.5 18.7 %copy-start = (bf16[16,128,64]{1,2,0:T(8,128)(2,1)S(1)}, bf16[16,128,64]{1,2,0:T(8,128)(2,1)}, u32[]{:S(2)}) copy-start(bf16[16,128,64]{1,2,0:T(8,128)(2,1)} %param.13) | copy-start | bytes 786436
  6.5 31.4 %copy-start.1 = (bf16[16,128,64]{1,2,0:T(8,128)(2,1)S(1)}, bf16[16,128,64]{1,2,0:T(8,128)(2,1)}, u32[]{:S(2)}) copy-start(bf16[16,128,64]{1,2,0:T(8,128)(2,1)} %param.14) | copy-start | bytes 786436
  26.9 32.1 %copy-start.7 = (s32[16]{0:T(128)S(1)}, s32[16]{0:T(128)}, u32[]{:S(2)}) copy-start(s32[16]{0:T(128)} %param.16) | copy-start | bytes 196
  26.9 28.1 %all-to-all-start.1 = ((bf16[32,2,128,64]{2,3,1,0:T(8,128)(2,1)}), bf16[32,2,128,64]{2,3,1,0:T(8,128)(2,1)S(1)}, u32[]{:S(2)}, u32[]{:S(2)}) async-start(bf16[32,2,128,64]{2,3,1,0:T(8,128)(2,1)} %bitcast.4), calls=%async_computation.1 | async-start | bytes 2097152 | tf_op jit(solution)/shard_map/all_to_all | solution.py:104
  37.9 21.9 %copy-start.2 = (bf16[16,16,64]{2,1,0:T(8,128)(2,1)S(1)}, bf16[16,16,64]{2,1,0:T(8,128)(2,1)}, u32[]{:S(2)}) copy-start(bf16[16,16,64]{2,1,0:T(8,128)(2,1)} %param.10) | copy-start | bytes 98308
  37.9 24.0 %copy-start.6 = (bf16[16,64]{1,0:T(8,128)(2,1)S(1)}, bf16[16,64]{1,0:T(8,128)(2,1)}, u32[]{:S(2)}) copy-start(bf16[16,64]{1,0:T(8,128)(2,1)} %param.11) | copy-start | bytes 6148
  38.0 27.5 %copy-start.3 = (bf16[16,64]{1,0:T(8,128)(2,1)S(1)}, bf16[16,64]{1,0:T(8,128)(2,1)}, u32[]{:S(2)}) copy-start(bf16[16,64]{1,0:T(8,128)(2,1)} %param.12) | copy-start | bytes 6148
  38.0 27.5 %copy-start.4 = (bf16[16,64]{1,0:T(8,128)(2,1)S(1)}, bf16[16,64]{1,0:T(8,128)(2,1)}, u32[]{:S(2)}) copy-start(bf16[16,64]{1,0:T(8,128)(2,1)} %param.18) | copy-start | bytes 6148
  38.0 39.2 %copy-start.5 = (bf16[16,16,64]{2,1,0:T(8,128)(2,1)S(1)}, bf16[16,16,64]{2,1,0:T(8,128)(2,1)}, u32[]{:S(2)}) copy-start(bf16[16,16,64]{2,1,0:T(8,128)(2,1)} %param.17) | copy-start | bytes 98308
  55.0 21.1 %all-to-all-start = ((bf16[32,2,128,64]{2,3,1,0:T(8,128)(2,1)}), bf16[32,2,128,64]{2,3,1,0:T(8,128)(2,1)S(1)}, u32[]{:S(2)}, u32[]{:S(2)}) async-start(bf16[32,2,128,64]{2,3,1,0:T(8,128)(2,1)} %bitcast.2), calls=%async_computation | async-start | bytes 2097152 | tf_op jit(solution)/shard_map/all_to_all | solution.py:105
  59.0 149.4 %reduce-scatter.2.cloned.1.call-start = ((), (), s32[]{:S(2)}) async-start(), calls=%async_computation.4 | async-start | bytes 4456448 | tf_op jit(solution)/shard_map/reduce_scatter | solution.py:120
  60.0 16.7 %collective-permute-start = (f32[16,16,1,128]{3,1,0,2:T(8,128)S(1)}, f32[16,16,1,128]{3,1,0,2:T(8,128)S(1)}, u32[]{:S(2)}, u32[]{:S(2)}) collective-permute-start(f32[16,16,1,128]{3,1,0,2:T(8,128)S(1)} %convolution_bitcast_fusion), channel_id=1, source_target_pairs={{0,1},{1,0},{2,3},{3,2},{4,5},{5,4},{6,7},{7,6},{8,9},{9,8},{10,11... | collective-permute-start | bytes 393224 | tf_op jit(solution)/shard_map/ppermute | solution.py:19
  62.1 14.8 %collective-permute-start.1 = (f32[16,16,1]{1,0,2:T(8,128)S(1)}, f32[16,16,1]{1,0,2:T(8,128)S(1)}, u32[]{:S(2)}, u32[]{:S(2)}) collective-permute-start(f32[16,16,1]{1,0,2:T(8,128)S(1)} %bitcast.77), channel_id=1, source_target_pairs={{0,1},{1,0},{2,3},{3,2},{4,5},{5,4},{6,7},{7,6},{8,9},{9,8},{10,11... | collective-permute-start | bytes 3080 | tf_op jit(solution)/shard_map/ppermute | solution.py:19
Sparse Core Ops, SparseCore 0:
  145.7 62.5 reduce-scatter.1
